TPU v7x, 512 devices: a whole 4x4x16 slice. The times are simulated.
512 devices in a mesh: kv: 8 (over y, core), pages: 64 (over x, z).
Axes of the slice: x: 4, y: 4, z: 16, core: 2. Of those that a mesh axis runs over, the one named last changes fastest.
Arguments:
- tokens: int32 [2, 64], replicated, may hold values from 0 to 31999
- prompt_len: int32 [8], replicated, may hold values from 193 to 8192, as said below
- page_table: int32 [8, 64], replicated, may hold values from -1 to 511, as said below
- parents: int32 [2, 64], replicated, may hold values from 0 to 63, as said below
- embedding: bfloat16 [32000, 7168], P('kv', 'pages'), may hold values from -6 to 6
- norm_gain: bfloat16 [7168], P('pages'), may hold values from 0.099609375 to 1.8984375
- w_qkv: bfloat16 [7168, 9216], P('pages', 'kv'), may hold values from -0.0625 to 0.0625
- w_out: bfloat16 [7168, 7168], P('kv', 'pages'), may hold values from -0.8984375 to 0.8984375
- history: bfloat16 [2, 64, 13, 1024], P(None, None, None, 'kv'), may hold values from -6 to 6
- kv_pool: bfloat16 [2, 512, 128, 1024], P(None, 'pages', None, 'kv'), may hold values from -400 to 400
Outputs:
- hidden: bfloat16 [2, 64, 7168], P(None, None, 'pages')
- history_out: bfloat16 [2, 64, 15, 1024], P(None, None, None, 'kv')
Inputs may be any that keep to these rules, and one draw needn't show every extreme that they name: `prompt_len`: each prompt is either long, within 512 tokens below 8192, or short, within 64 tokens below 256; some group's prompt has exactly 8192 tokens. For j below prompt_len[g] / 128 rounded up, page_table[g, j] is the slot holding tokens j * 128 to j * 128 + 127 of group g's prompt; no slot is named twice; all other entries are -1. parents[t, b] is a beam of b's group; at the first step the first and the last beam of every group continue their own history.
All inputs are finite; a program needn't handle non-finite values.
Results may differ from a plain program's by a relative error of at most 0.015.
The roundings to bfloat16 on the way count: a program that leaves them out, or rounds other values in their place, can miss the bound.
Values may be sent and summed in bfloat16 or wider, within the bound.
No kernel may reach another device: no remote copies, remote signals or barrier semaphores. Data moves between devices by JAX's collectives and lax.ppermute only.
A program may use at most 128 MiB of HBM per device.

v0:
```python
import jax
import jax.numpy as jnp
from jax import lax
from jax.sharding import PartitionSpec as P

D = 7168
KV_HEADS = 8
HEAD_DIM = 128
GROUPS = 8
BEAMS = 8
PRIOR = 13
PAGE = 128
PER_KV = 7
HISTORY = 15
MAX_PAGES = 64
THETA = 5000000.0
EPSILON = 1e-05
NEGATIVE = -1e30


def rotate(values, positions):
    half_dim = HEAD_DIM // 2
    frequency = THETA ** (-(2.0 * jnp.arange(half_dim, dtype=jnp.float32)) / HEAD_DIM)
    angles = positions.astype(jnp.float32)[:, None] * frequency[None, :]
    cosine = jnp.cos(angles)[:, None, None, :]
    sine_part = jnp.sin(angles)[:, None, None, :]
    lower_part = values[..., :half_dim]
    upper_part = values[..., half_dim:]
    return jnp.concatenate(
        [
            lower_part * cosine - upper_part * sine_part,
            upper_part * cosine + lower_part * sine_part,
        ],
        axis=-1,
    )


def finish_rows(summed, norm_sums, row_ids, prompt_len, num_seqs, local_heads):
    inverse_rms = lax.rsqrt(norm_sums / D + EPSILON)
    projected = (summed * inverse_rms[:, None]).reshape(-1, local_heads, PER_KV + 2, HEAD_DIM)
    positions = jnp.take(prompt_len, row_ids % num_seqs // BEAMS) + PRIOR + row_ids // num_seqs
    turned = rotate(projected[:, :, : PER_KV + 1], positions)
    return jnp.concatenate([turned, projected[:, :, PER_KV + 1 :]], axis=2).astype(jnp.bfloat16)


def combine(earlier, later):
    peak = jnp.maximum(earlier[0], later[0])
    weight_one = jnp.exp(earlier[0] - peak)
    weight_two = jnp.exp(later[0] - peak)
    return (
        peak,
        earlier[1] * weight_one + later[1] * weight_two,
        earlier[2] * weight_one[:, None] + later[2] * weight_two[:, None],
    )


def reduce_rows(packed, axis):
    sources = lax.axis_size(axis)
    split = packed.reshape(sources, packed.shape[0] // sources, *packed.shape[1:])
    return jnp.sum(lax.all_to_all(split, axis, 0, 0, tiled=False), axis=0)


def per_device(
    tokens, prompt_len, page_table, parents, embedding, norm_gain, w_qkv, w_out, history, kv_pool
):
    num_steps, num_seqs = tokens.shape
    row_count = num_steps * num_seqs
    page_devices = lax.axis_size("pages")
    page_index = lax.axis_index("pages")
    local_heads = KV_HEADS // lax.axis_size("kv")
    kv_width = local_heads * HEAD_DIM
    inv_root = 1.0 / jnp.sqrt(jnp.float32(HEAD_DIM))
    vocab_local = embedding.shape[0]
    local_ids = tokens.reshape(-1) - lax.axis_index("kv") * vocab_local
    inside = (local_ids >= 0) & (local_ids < vocab_local)
    picked = jnp.take(embedding, jnp.clip(local_ids, 0, vocab_local - 1), axis=0)
    found = jnp.where(inside[:, None], picked, jnp.zeros_like(picked))
    embedded = lax.psum(found, "kv")
    widened = embedded.astype(jnp.float32)
    squares = jnp.sum(widened * widened, axis=1)
    normed = (widened * norm_gain.astype(jnp.float32)).astype(jnp.bfloat16)
    partial_value = jnp.dot(normed, w_qkv, preferred_element_type=jnp.float32)
    qkv_cols = partial_value.shape[1]
    packed = jnp.concatenate(
        [partial_value, squares[:, None], jnp.zeros((row_count, 127), jnp.float32)], axis=1
    )
    reduced = reduce_rows(packed, "pages")
    rows_per = row_count // page_devices
    my_rows = page_index * rows_per + jnp.arange(rows_per, dtype=jnp.int32)
    mine = finish_rows(
        reduced[:, :qkv_cols], reduced[:, qkv_cols], my_rows, prompt_len, num_seqs, local_heads
    )
    projected = lax.all_gather(
        mine.reshape(rows_per, qkv_cols), "pages", axis=0, tiled=True
    ).reshape(row_count, local_heads, PER_KV + 2, HEAD_DIM)
    queries = projected[:, :, :PER_KV]
    fresh_kv = jnp.stack([projected[:, :, PER_KV], projected[:, :, PER_KV + 1]]).reshape(
        2, num_steps, num_seqs, kv_width
    )
    buffer = jnp.concatenate(
        [history, jnp.zeros((2, num_seqs, num_steps, kv_width), jnp.bfloat16)], axis=2
    )
    snapshots = []
    for step_index in range(num_steps):
        buffer = jnp.take(buffer, parents[step_index], axis=1)
        buffer = buffer.at[:, :, PRIOR + step_index].set(fresh_kv[:, step_index])
        snapshots.append(buffer)
    stacked = jnp.stack(snapshots)
    tail_keys = stacked[:, 0].reshape(num_steps, num_seqs, HISTORY, local_heads, HEAD_DIM)
    tail_vals = stacked[:, 1].reshape(num_steps, num_seqs, HISTORY, local_heads, HEAD_DIM)
    step_query = queries.reshape(num_steps, num_seqs, local_heads, PER_KV, HEAD_DIM)
    tail_len = PRIOR + 1 + jnp.arange(num_steps, dtype=jnp.int32)
    tail_valid = (jnp.arange(HISTORY, dtype=jnp.int32)[None, :] < tail_len[:, None])[
        :, None, None, None, :
    ]
    tail_scores = (
        jnp.einsum("tbkhd,tblkd->tbkhl", step_query, tail_keys, preferred_element_type=jnp.float32)
        * inv_root
    )
    tail_scores = jnp.where(tail_valid, tail_scores, NEGATIVE)
    tail_peak = jnp.max(tail_scores, axis=-1)
    tail_exp = jnp.where(tail_valid, jnp.exp(tail_scores - tail_peak[..., None]), 0.0)
    tail_total = jnp.sum(tail_exp, axis=-1)
    tail_acc = jnp.einsum(
        "tbkhl,tblkd->tbkhd",
        tail_exp.astype(jnp.bfloat16),
        tail_vals,
        preferred_element_type=jnp.float32,
    )
    tail_part = (tail_peak.reshape(-1), tail_total.reshape(-1), tail_acc.reshape(-1, HEAD_DIM))
    slot_rows = kv_pool.shape[1]
    slot_ids = page_index * slot_rows + jnp.arange(slot_rows, dtype=jnp.int32)
    matches = page_table[:, :, None] == slot_ids[None, None, :]
    slot_used = jnp.any(matches, axis=(0, 1))
    owner_group = jnp.sum(
        jnp.where(matches, jnp.arange(GROUPS, dtype=jnp.int32)[:, None, None], 0), axis=(0, 1)
    )
    page_number = jnp.sum(
        jnp.where(matches, jnp.arange(MAX_PAGES, dtype=jnp.int32)[None, :, None], 0), axis=(0, 1)
    )
    length = jnp.take(prompt_len, owner_group)
    live_tok = slot_used[:, None] & (
        page_number[:, None] * PAGE + jnp.arange(PAGE, dtype=jnp.int32)[None, :] < length[:, None]
    )
    live_full = live_tok[None, :, None, :]
    grouped = queries.reshape(num_steps, GROUPS, BEAMS, local_heads, PER_KV, HEAD_DIM)
    chosen = jnp.take(grouped, owner_group, axis=1)
    query_rows = num_steps * BEAMS * PER_KV
    chosen = jnp.transpose(chosen, (3, 1, 0, 2, 4, 5)).reshape(
        local_heads, slot_rows, query_rows, HEAD_DIM
    )
    page_keys = jnp.transpose(
        kv_pool[0].reshape(slot_rows, PAGE, local_heads, HEAD_DIM), (2, 0, 1, 3)
    )
    page_vals = jnp.transpose(
        kv_pool[1].reshape(slot_rows, PAGE, local_heads, HEAD_DIM), (2, 0, 1, 3)
    )
    scores = (
        jnp.einsum("ksqd,kspd->ksqp", chosen, page_keys, preferred_element_type=jnp.float32)
        * inv_root
    )
    scores = jnp.where(live_full, scores, NEGATIVE)
    slot_peak = jnp.max(scores, axis=-1)
    slot_exp = jnp.where(live_full, jnp.exp(scores - slot_peak[..., None]), 0.0)
    slot_total = jnp.sum(slot_exp, axis=-1)
    slot_acc = jnp.einsum(
        "ksqp,kspd->ksqd",
        slot_exp.astype(jnp.bfloat16),
        page_vals,
        preferred_element_type=jnp.float32,
    )
    member = (owner_group[:, None] == jnp.arange(GROUPS, dtype=jnp.int32)[None, :]) & slot_used[
        :, None
    ]
    spread = jnp.where(member[None, :, :, None], slot_peak[:, :, None, :], NEGATIVE)
    group_peak = jnp.max(spread, axis=1)
    slot_base = jnp.take(group_peak, owner_group, axis=1)
    weight = jnp.where(slot_used[None, :, None], jnp.exp(slot_peak - slot_base), 0.0)
    member_f = member.astype(jnp.float32)
    group_total = jnp.einsum(
        "sg,ksq->kgq", member_f, slot_total * weight, precision=lax.Precision.HIGHEST
    )
    group_acc = jnp.einsum(
        "sg,ksqd->kgqd", member_f, slot_acc * weight[..., None], precision=lax.Precision.HIGHEST
    )
    order_small = (2, 1, 3, 0, 4)
    peak_rows = jnp.transpose(
        group_peak.reshape(local_heads, GROUPS, num_steps, BEAMS, PER_KV), order_small
    )
    total_rows = jnp.transpose(
        group_total.reshape(local_heads, GROUPS, num_steps, BEAMS, PER_KV), order_small
    )
    acc_rows = jnp.transpose(
        group_acc.reshape(local_heads, GROUPS, num_steps, BEAMS, PER_KV, HEAD_DIM),
        (2, 1, 3, 0, 4, 5),
    )
    local_part = (peak_rows.reshape(-1), total_rows.reshape(-1), acc_rows.reshape(-1, HEAD_DIM))
    with_tail = combine(local_part, tail_part)
    first = page_index == 0
    part = jax.tree.map(lambda a, b: jnp.where(first, a, b), with_tail, local_part)
    attn_rows = part[0].shape[0]
    share = attn_rows // page_devices
    stats = jnp.zeros((page_devices, 2, HEAD_DIM), jnp.float32)
    stats = stats.at[:, 0, :share].set(part[0].reshape(page_devices, share))
    stats = stats.at[:, 1, :share].set(part[1].reshape(page_devices, share))
    sent = jnp.concatenate([part[2].reshape(page_devices, share, HEAD_DIM), stats], axis=1)
    received = lax.all_to_all(sent, "pages", 0, 0, tiled=False)
    src_acc = received[:, :share]
    src_peak = received[:, share, :share]
    src_total = received[:, share + 1, :share]
    top = jnp.max(src_peak, axis=0)
    scale = jnp.exp(src_peak - top[None, :])
    total = jnp.sum(src_total * scale, axis=0)
    acc = jnp.sum(src_acc * scale[:, :, None], axis=0)
    attended_mine = (acc / total[:, None]).astype(jnp.bfloat16)
    attended = lax.all_gather(attended_mine, "pages", axis=0, tiled=True)
    flat_heads = attended.reshape(row_count, local_heads * PER_KV * HEAD_DIM)
    head_terms = jnp.dot(flat_heads, w_out, preferred_element_type=jnp.float32)
    mixed_out = lax.psum(head_terms, "kv") + widened
    return (mixed_out.astype(jnp.bfloat16).reshape(num_steps, num_seqs, -1), buffer)


def solution(mesh):
    placed = (
        P(),
        P(),
        P(),
        P(),
        P("kv", "pages"),
        P("pages"),
        P("pages", "kv"),
        P("kv", "pages"),
        P(None, None, None, "kv"),
        P(None, "pages", None, "kv"),
    )
    return jax.shard_map(
        per_device,
        mesh=mesh,
        in_specs=placed,
        out_specs=(P(None, None, "pages"), P(None, None, None, "kv")),
        check_vma=False,
    )
```

profile of v0, /device:TPU:2, one launch (start us, length us, event | category | flops | bytes accessed | tf_op | source)
XLA Modules:
  0.0 330.2 jit_solution(9333004491464431049)
XLA Ops:
  0.7 0.7 copy-done.6
  2.2 1.9 copy.207
  4.2 0.7 gather_fusion.1
  5.0 25.9 %psum.14 = bf16[128,112]{0,1:T(8,128)(2,1)S(1)} all-reduce(bf16[128,112]{0,1:T(8,128)(2,1)S(1)} %select_select_fusion), channel_id=1, replica_groups=mesh['kv'=8,'pages'=64] {'kv'}, use_global_device_ids=true, to_apply=%region_3.4 | all-reduce | flops 14336 | bytes 57344 | tf_op jit(solution)/shard_map/psum | solution.py:78
  31.9 2.2 concatenate.36
  34.1 18.8 %all-to-all-start = ((f32[64,2,1280]{2,1,0:T(2,128)}), f32[64,2,1280]{2,1,0:T(2,128)S(1)}, u32[]{:S(2)}, u32[]{:S(2)}) async-start(f32[64,2,1280]{2,1,0:T(2,128)} %concatenate.36), calls=%async_computation | async-start | bytes 1310720 | tf_op jit(solution)/shard_map/all_to_all | solution.py:60
  52.9 0.7 copy-done.5
  54.1 0.6 gather_fusion
  54.8 0.6 gather_fusion.2
  56.6 1.6 gather_fusion.5
  58.6 28.0 %all-to-all-done = f32[64,2,1280]{2,1,0:T(2,128)S(1)} async-done(((f32[64,2,1280]{2,1,0:T(2,128)}), f32[64,2,1280]{2,1,0:T(2,128)S(1)}, u32[]{:S(2)}, u32[]{:S(2)}) %all-to-all-start) | async-done | bytes 655392 | tf_op jit(solution)/shard_map/all_to_all | solution.py:60
  87.2 94.1 %all-gather = bf16[64,2,1152]{2,1,0:T(2,128)(2,1)S(1)} all-gather(bf16[1,2,1152]{2,1,0:T(2,128)(2,1)S(1)} %reshape.977), channel_id=1, replica_groups=mesh['kv'=8,'pages'=64] {'pages'}, dimensions={0}, use_global_device_ids=true | all-gather | bytes 299520 | tf_op jit(solution)/shard_map/all_gather | solution.py:93
  181.7 0.6 gather_fusion.3
  182.5 0.9 copy-done.4
  184.7 1.4 scatter.14
  186.6 1.6 gather_fusion.6
  192.6 0.9 pad_maximum_fusion.1
  193.5 8.4 %all-to-all-start.1 = ((f32[64,16,128]{2,1,0:T(8,128)}), f32[64,16,128]{2,1,0:T(8,128)S(1)}, u32[]{:S(2)}, u32[]{:S(2)}) async-start(f32[64,16,128]{2,1,0:T(8,128)} %pad_maximum_fusion.1), calls=%async_computation.1 | async-start | bytes 1048576 | tf_op jit(solution)/shard_map/all_to_all | solution.py:207
  201.9 0.9 copy.237
  202.8 20.7 %all-to-all-done.1 = f32[64,16,128]{2,1,0:T(8,128)S(1)} async-done(((f32[64,16,128]{2,1,0:T(8,128)}), f32[64,16,128]{2,1,0:T(8,128)S(1)}, u32[]{:S(2)}, u32[]{:S(2)}) %all-to-all-start.1) | async-done | bytes 524320 | tf_op jit(solution)/shard_map/all_to_all | solution.py:207
  223.9 80.4 %all-gather.1 = bf16[64,14,128]{2,1,0:T(8,128)(2,1)S(1)} all-gather(bf16[1,14,128]{2,1,0:T(8,128)(2,1)S(1)} %fusion.46), channel_id=1, replica_groups=mesh['kv'=8,'pages'=64] {'pages'}, dimensions={0}, use_global_device_ids=true | all-gather | bytes 232960 | tf_op jit(solution)/shard_map/all_gather | solution.py:216
  304.6 0.7 copy-done.3
  305.5 24.0 %psum.15 = f32[128,112]{0,1:T(8,128)S(1)} all-reduce(f32[128,112]{0,1:T(8,128)S(1)} %fusion.67), channel_id=1, replica_groups=mesh['kv'=8,'pages'=64] {'kv'}, use_global_device_ids=true, to_apply=%region_14.16 | all-reduce | flops 14336 | bytes 114688 | tf_op jit(solution)/shard_map/psum | solution.py:219
  329.5 0.7 copy.236
  (114 shorter events, 12.2 us)
Async XLA Ops:
  0.6 30.6 %copy-start = (bf16[112,1152]{1,0:T(8,128)(2,1)S(1)}, bf16[112,1152]{1,0:T(8,128)(2,1)}, u32[]{:S(2)}) copy-start(bf16[112,1152]{1,0:T(8,128)(2,1)} %param.26) | copy-start | bytes 774148
  0.7 0.7 copy-start.6
  1.5 0.7 copy-start.8
  34.1 20.0 %copy-start.1 = (s32[8]{0:T(128)S(1)}, s32[8]{0:T(128)}, u32[]{:S(2)}) copy-start(s32[8]{0:T(128)} %param.21) | copy-start | bytes 100
  34.1 52.5 %all-to-all-start = ((f32[64,2,1280]{2,1,0:T(2,128)}), f32[64,2,1280]{2,1,0:T(2,128)S(1)}, u32[]{:S(2)}, u32[]{:S(2)}) async-start(f32[64,2,1280]{2,1,0:T(2,128)} %concatenate.36), calls=%async_computation | async-start | bytes 1310720 | tf_op jit(solution)/shard_map/all_to_all | solution.py:60
  52.9 0.7 copy-start.5
  54.1 1.3 copy-start.2
  55.9 0.7 copy-start.7
  182.3 1.0 copy-start.4
  193.5 30.1 %all-to-all-start.1 = ((f32[64,16,128]{2,1,0:T(8,128)}), f32[64,16,128]{2,1,0:T(8,128)S(1)}, u32[]{:S(2)}, u32[]{:S(2)}) async-start(f32[64,16,128]{2,1,0:T(8,128)} %pad_maximum_fusion.1), calls=%async_computation.1 | async-start | bytes 1048576 | tf_op jit(solution)/shard_map/all_to_all | solution.py:207
  304.3 0.9 copy-start.3
where the time goes:
time: 331 us; the launch traced here: 330 us
  blocking collectives  224 us (68%)
  waiting for transfers between devices  48.7 us (15%)
  starting transfers between devices  27.2 us (8%)
  local copies, waits for them, and re-layouts  21.8 us (7%)
  other arithmetic  4.29 us (1%)
    all_gather x1, blocking collectives, per_device(): lax.all_gather(mine.reshape(rows_per, qkv_cols), 'pages', axis=0, tiled=T...  94.1 us
    all_gather x1, blocking collectives, per_device(): attended = lax.all_gather(attended_mine, 'pages', axis=0, tiled=True)  80.4 us
    all_to_all x1, waiting for transfers between devices, reduce_rows(): return jnp.sum(lax.all_to_all(split, axis, 0, 0, tiled=False), axis=0)  28 us
    psum x1, blocking collectives, per_device(): embedded = lax.psum(found, 'kv')  25.9 us
    psum x1, blocking collectives, per_device(): mixed_out = lax.psum(head_terms, 'kv') + widened  24 us
    all_to_all x1, waiting for transfers between devices, per_device(): received = lax.all_to_all(sent, 'pages', 0, 0, tiled=False)  20.7 us
    all_to_all x1, starting transfers between devices, reduce_rows(): return jnp.sum(lax.all_to_all(split, axis, 0, 0, tiled=False), axis=0)  18.8 us
    all_to_all x1, starting transfers between devices, per_device(): received = lax.all_to_all(sent, 'pages', 0, 0, tiled=False)  8.39 us
  transfers between devices with their start and end apart: 2, of which 2 were waited for; matrix products, arithmetic and copies ran while one was open for 2% of the time, Pallas kernels for 0%

commit v1 on v0

--- a/solution.py
+++ b/solution.py
@@ -213,7 +213,9 @@
     total = jnp.sum(src_total * scale, axis=0)
     acc = jnp.sum(src_acc * scale[:, :, None], axis=0)
     attended_mine = (acc / total[:, None]).astype(jnp.bfloat16)
-    attended = lax.all_gather(attended_mine, "pages", axis=0, tiled=True)
+    attended = jnp.concatenate(
+        lax.all_to_all(jnp.stack([attended_mine] * lax.axis_size("pages")), "pages", 0, 0), axis=0
+    )
     flat_heads = attended.reshape(row_count, local_heads * PER_KV * HEAD_DIM)
     head_terms = jnp.dot(flat_heads, w_out, preferred_element_type=jnp.float32)
     mixed_out = lax.psum(head_terms, "kv") + widened

time: 331 us -> 279 us (0.84)
  the two profiles are of different devices: /device:TPU:2 before, /device:TPU:6 now
where the time goes in v1:
time: 279 us; the launch traced here: 278 us
  blocking collectives  179 us (64%)
  waiting for transfers between devices  43.6 us (16%)
  starting transfers between devices  25.9 us (9%)
  local copies, waits for them, and re-layouts  21.9 us (8%)
  other arithmetic  3.5 us (1%)
    all_gather x1, blocking collectives, per_device(): lax.all_gather(mine.reshape(rows_per, qkv_cols), 'pages', axis=0, tiled=T...  93.6 us
    all_to_all x1, blocking collectives, per_device(): received = lax.all_to_all(sent, 'pages', 0, 0, tiled=False)  34.7 us
    all_to_all x1, waiting for transfers between devices, reduce_rows(): return jnp.sum(lax.all_to_all(split, axis, 0, 0, tiled=False), axis=0)  28 us
    psum x1, blocking collectives, per_device(): embedded = lax.psum(found, 'kv')  25.9 us
    psum x1, blocking collectives, per_device(): mixed_out = lax.psum(head_terms, 'kv') + widened  25.2 us
    all_to_all x1, starting transfers between devices, reduce_rows(): return jnp.sum(lax.all_to_all(split, axis, 0, 0, tiled=False), axis=0)  18.9 us
    all_to_all x1, waiting for transfers between devices, per_device(): lax.all_to_all(jnp.stack([attended_mine] * lax.axis_size('pages')), 'page...  15.6 us
    all_to_all x1, starting transfers between devices, per_device(): lax.all_to_all(jnp.stack([attended_mine] * lax.axis_size('pages')), 'page...  7.02 us
  transfers between devices with their start and end apart: 2, of which 2 were waited for; matrix products, arithmetic and copies ran while one was open for 2% of the time, Pallas kernels for 0%

profile of v1, /device:TPU:6, one launch (start us, length us, event | category | flops | bytes accessed | tf_op | source)
XLA Modules:
  0.0 278.2 jit_solution(8428687050331847994)
XLA Ops:
  0.7 0.7 copy-done.6
  1.6 0.6 copy-done.8
  2.2 1.9 copy.207
  4.2 0.7 gather_fusion.1
  5.0 25.9 %psum.14 = bf16[128,112]{0,1:T(8,128)(2,1)S(1)} all-reduce(bf16[128,112]{0,1:T(8,128)(2,1)S(1)} %select_select_fusion), channel_id=1, replica_groups=mesh['kv'=8,'pages'=64] {'kv'}, use_global_device_ids=true, to_apply=%region_3.4 | all-reduce | flops 14336 | bytes 57344 | tf_op jit(solution)/shard_map/psum | solution.py:78
  31.9 2.2 concatenate.36
  34.1 18.9 %all-to-all-start = ((f32[64,2,1280]{2,1,0:T(2,128)}), f32[64,2,1280]{2,1,0:T(2,128)S(1)}, u32[]{:S(2)}, u32[]{:S(2)}) async-start(f32[64,2,1280]{2,1,0:T(2,128)} %concatenate.36), calls=%async_computation | async-start | bytes 1310720 | tf_op jit(solution)/shard_map/all_to_all | solution.py:60
  53.1 0.7 copy-done.5
  54.3 0.6 gather_fusion
  54.9 0.6 gather_fusion.2
  56.7 1.6 gather_fusion.5
  58.8 28.0 %all-to-all-done = f32[64,2,1280]{2,1,0:T(2,128)S(1)} async-done(((f32[64,2,1280]{2,1,0:T(2,128)}), f32[64,2,1280]{2,1,0:T(2,128)S(1)}, u32[]{:S(2)}, u32[]{:S(2)}) %all-to-all-start) | async-done | bytes 655392 | tf_op jit(solution)/shard_map/all_to_all | solution.py:60
  87.4 93.6 %all-gather = bf16[64,2,1152]{2,1,0:T(2,128)(2,1)S(1)} all-gather(bf16[1,2,1152]{2,1,0:T(2,128)(2,1)S(1)} %reshape.981), channel_id=1, replica_groups=mesh['kv'=8,'pages'=64] {'pages'}, dimensions={0}, use_global_device_ids=true | all-gather | bytes 299520 | tf_op jit(solution)/shard_map/all_gather | solution.py:93
  181.4 0.6 gather_fusion.3
  182.1 0.9 copy-done.4
  184.4 1.4 scatter.14
  186.3 1.6 gather_fusion.6
  192.3 34.7 %all_to_all.15 = f32[64,16,128]{2,1,0:T(8,128)S(1)} all-to-all(f32[64,16,128]{2,1,0:T(8,128)S(1)} %pad_maximum_fusion.1), channel_id=1, replica_groups=mesh['kv'=8,'pages'=64] {'pages'}, dimensions={0} | all-to-all | bytes 1048576 | tf_op jit(solution)/shard_map/all_to_all | solution.py:207
  227.5 0.7 stack.20
  228.2 7.0 %all-to-all-start.2 = ((bf16[64,14,128]{2,1,0:T(8,128)(2,1)}), bf16[64,14,128]{2,1,0:T(8,128)(2,1)S(1)}, u32[]{:S(2)}, u32[]{:S(2)}) async-start(bf16[64,14,128]{2,1,0:T(8,128)(2,1)} %stack.20), calls=%async_computation.2 | async-start | bytes 524288 | tf_op jit(solution)/shard_map/all_to_all | solution.py:217
  235.2 0.9 copy.237
  236.1 15.6 %all-to-all-done.2 = bf16[64,14,128]{2,1,0:T(8,128)(2,1)S(1)} async-done(((bf16[64,14,128]{2,1,0:T(8,128)(2,1)}), bf16[64,14,128]{2,1,0:T(8,128)(2,1)S(1)}, u32[]{:S(2)}, u32[]{:S(2)}) %all-to-all-start.2) | async-done | bytes 229408 | tf_op jit(solution)/shard_map/all_to_all | solution.py:217
  252.2 25.2 %psum.15 = f32[128,112]{0,1:T(8,128)S(1)} all-reduce(f32[128,112]{0,1:T(8,128)S(1)} %fusion.66), channel_id=1, replica_groups=mesh['kv'=8,'pages'=64] {'kv'}, use_global_device_ids=true, to_apply=%region_14.16 | all-reduce | flops 14336 | bytes 114688 | tf_op jit(solution)/shard_map/psum | solution.py:221
  277.4 0.7 copy.236
  (115 shorter events, 11.7 us)
Async XLA Ops:
  0.6 30.6 %copy-start = (bf16[112,1152]{1,0:T(8,128)(2,1)S(1)}, bf16[112,1152]{1,0:T(8,128)(2,1)}, u32[]{:S(2)}) copy-start(bf16[112,1152]{1,0:T(8,128)(2,1)} %param.26) | copy-start | bytes 774148
  0.7 0.7 copy-start.6
  1.5 0.7 copy-start.8
  34.1 20.1 %copy-start.1 = (s32[8]{0:T(128)S(1)}, s32[8]{0:T(128)}, u32[]{:S(2)}) copy-start(s32[8]{0:T(128)} %param.21) | copy-start | bytes 100
  34.1 52.6 %all-to-all-start = ((f32[64,2,1280]{2,1,0:T(2,128)}), f32[64,2,1280]{2,1,0:T(2,128)S(1)}, u32[]{:S(2)}, u32[]{:S(2)}) async-start(f32[64,2,1280]{2,1,0:T(2,128)} %concatenate.36), calls=%async_computation | async-start | bytes 1310720 | tf_op jit(solution)/shard_map/all_to_all | solution.py:60
  53.0 0.7 copy-start.5
  54.2 1.3 copy-start.2
  56.0 0.7 copy-start.7
  182.0 1.0 copy-start.4
  228.2 23.6 %all-to-all-start.2 = ((bf16[64,14,128]{2,1,0:T(8,128)(2,1)}), bf16[64,14,128]{2,1,0:T(8,128)(2,1)S(1)}, u32[]{:S(2)}, u32[]{:S(2)}) async-start(bf16[64,14,128]{2,1,0:T(8,128)(2,1)} %stack.20), calls=%async_computation.2 | async-start | bytes 524288 | tf_op jit(solution)/shard_map/all_to_all | solution.py:217
  236.1 15.9 %copy-start.3 = (bf16[896,112]{0,1:T(8,128)(2,1)S(1)}, bf16[896,112]{0,1:T(8,128)(2,1)}, u32[]{:S(2)}) copy-start(bf16[896,112]{0,1:T(8,128)(2,1)} %param.27) | copy-start | bytes 602116
